TPU v7x, 256 devices: a whole 4x4x8 slice. The times are simulated.
256 devices in a mesh: embed: 8 (over x, core), hidden: 32 (over y, z).
Axes of the slice: x: 4, y: 4, z: 8, core: 2. Of those that a mesh axis runs over, the one named last changes fastest.
Arguments:
- rows_in: bfloat16 [512, 16384], P('hidden', 'embed'), may hold values from -6 to 6
- gate_weight: bfloat16 [16384, 28672], P('embed', 'hidden'), may hold values from -0.046875 to 0.046875
- up_weight: bfloat16 [16384, 28672], P('embed', 'hidden'), may hold values from -0.046875 to 0.046875
- down_weight: bfloat16 [28672, 16384], P('hidden', 'embed'), may hold values from -0.03125 to 0.03125
Outputs:
- rows_out: bfloat16 [512, 16384], P('hidden', 'embed')
All inputs are finite; a program needn't handle non-finite values.
Results may differ from a plain program's by a relative error of at most 0.0049.
Values may be sent and summed in bfloat16 or wider, within the bound.
No kernel may reach another device: no remote copies, remote signals or barrier semaphores. Data moves between devices by JAX's collectives and lax.ppermute only.
A program may use at most 64 MiB of HBM per device.

v0:
```python
import jax
import jax.numpy as jnp
from jax import lax
from jax.sharding import Mesh, PartitionSpec as P


def on_device(rows_in, gate_weight, up_weight, down_weight):
    width = gate_weight.shape[1]
    piece = lax.all_gather(rows_in, "hz", axis=0, tiled=True)
    piece = lax.all_gather(piece, "hy", axis=0, tiled=True)
    gate_part = jnp.dot(piece, gate_weight, preferred_element_type=jnp.float32)
    up_part = jnp.dot(piece, up_weight, preferred_element_type=jnp.float32)
    partial_value = jnp.concatenate([gate_part, up_part], axis=1)
    summed = lax.psum_scatter(partial_value, "embed", scatter_dimension=0, tiled=True)
    activated = (jax.nn.silu(summed[:, :width]) * summed[:, width:]).astype(jnp.bfloat16)
    activated = lax.all_gather(activated, "embed", axis=0, tiled=True)
    partial_out = jnp.dot(activated, down_weight, preferred_element_type=jnp.float32)
    totals = lax.psum_scatter(partial_out, "hy", scatter_dimension=0, tiled=True)
    totals = lax.psum_scatter(totals, "hz", scatter_dimension=0, tiled=True)
    return totals.astype(jnp.bfloat16)


def solution(mesh):
    embed, hidden = (mesh.shape["embed"], mesh.shape["hidden"])
    ny = {d.coords[1] for d in mesh.devices.flat}
    ny = len(ny)
    sub = Mesh(mesh.devices.reshape(embed, ny, hidden // ny), ("embed", "hy", "hz"))
    rows = P(("hy", "hz"), "embed")
    weights = P("embed", ("hy", "hz"))
    placed = (rows, weights, weights, P(("hy", "hz"), "embed"))
    return jax.shard_map(on_device, mesh=sub, in_specs=placed, out_specs=rows, check_vma=False)
```

profile of v0, /device:TPU:2, one launch (start us, length us, event | category | flops | bytes accessed | tf_op | source)
XLA Modules:
  0.0 239.4 jit_solution(16744164856222922656)
XLA Ops:
  6.5 0.0 all-gather.2.cloned.1.call-start
  6.5 31.1 %all_gather.9 = bf16[128,2048]{1,0:T(8,128)(2,1)} all-gather(bf16[16,2048]{1,0:T(8,128)(2,1)} %param.4), channel_id=1, replica_groups=mesh['embed'=8,'hy'=4,'hz'=8] {'hz'}, dimensions={0}, use_global_device_ids=true | all-gather | bytes 589824 | tf_op jit(solution)/shard_map/all_gather | solution.py:9
  37.6 0.0 all-gather.2.cloned.1.call-update
  37.7 0.0 reduce-scatter.4.cloned.1.call-start
  37.7 33.1 %all-gather.2.cloned.1.call-done = bf16[512,2048]{1,0:T(8,128)(2,1)} async-done(((bf16[128,2048]{1,0:T(8,128)(2,1)}), bf16[512,2048]{1,0:T(8,128)(2,1)}) %all-gather.2.cloned.1.call-update) | async-done | bytes 2097168 | tf_op jit(solution)/shard_map/all_gather | solution.py:10
  70.8 0.0 copy-start
  70.8 0.0 copy-start.1
  70.8 5.1 %fusion.2 = f32[512,896]{1,0:T(8,128)S(1)} fusion(bf16[512,2048]{1,0:T(8,128)(2,1)} %all-gather.2.cloned.1.call-done, bf16[2048,896]{1,0:T(8,128)(2,1)} %param.6), kind=kOutput, calls=%fused_computation.4 | convolution fusion | flops 1879048192 | bytes 7602176 | tf_op jit(solution)/shard_map/dot_general | solution.py:12
  75.9 0.0 copy-done
  75.9 0.0 copy-done.1
  76.0 2.3 fusion.1
  78.3 2.1 pad_maximum_fusion
  80.3 0.0 reduce-scatter.4.cloned.1.call-update
  80.4 0.0 reduce-scatter.6.cloned.1.call-start
  80.4 36.1 %reduce-scatter.4.cloned.1.call-done = f32[64,1792]{1,0:T(8,128)} async-done(((f32[512,1792]{1,0:T(8,128)}), f32[64,1792]{1,0:T(8,128)}) %reduce-scatter.4.cloned.1.call-update) | async-done | bytes 458768 | tf_op jit(solution)/shard_map/reduce_scatter | solution.py:14
  116.5 1.1 fusion
  117.6 15.1 %all_gather.11 = bf16[512,896]{1,0:T(8,128)(2,1)S(1)} all-gather(bf16[64,896]{1,0:T(8,128)(2,1)S(1)} %fusion), channel_id=1, replica_groups=mesh['embed'=8,'hy'=4,'hz'=8] {'embed'}, dimensions={0}, use_global_device_ids=true | all-gather | bytes 1032192 | tf_op jit(solution)/shard_map/all_gather | solution.py:16
  132.7 6.3 %fusion.3 = f32[512,2048]{1,0:T(8,128)} fusion(bf16[512,896]{1,0:T(8,128)(2,1)S(1)} %all_gather.11, bf16[896,2048]{1,0:T(8,128)(2,1)} %param.7), kind=kOutput, calls=%fused_computation.5 | convolution fusion | flops 1879048192 | bytes 8781824 | tf_op jit(solution)/shard_map/dot_general | solution.py:17
  139.0 0.0 reduce-scatter.6.cloned.1.call-update
  139.1 0.0 reduce-scatter.8.cloned.1.call-start
  139.1 51.3 %reduce-scatter.6.cloned.1.call-done = f32[128,2048]{1,0:T(8,128)} async-done(((f32[512,2048]{1,0:T(8,128)}), f32[128,2048]{1,0:T(8,128)}) %reduce-scatter.6.cloned.1.call-update) | async-done | bytes 1048592 | tf_op jit(solution)/shard_map/reduce_scatter | solution.py:18
  190.4 0.0 reduce-scatter.8.cloned.1.call-update
  190.4 40.9 %reduce-scatter.8.cloned.1.call-done = f32[16,2048]{1,0:T(8,128)} async-done(((f32[128,2048]{1,0:T(8,128)}), f32[16,2048]{1,0:T(8,128)}) %reduce-scatter.8.cloned.1.call-update) | async-done | bytes 131088 | tf_op jit(solution)/shard_map/reduce_scatter | solution.py:19
  231.4 1.5 convert_element_type.7
Async XLA Ops:
  6.5 64.2 %all-gather.2.cloned.1.call-start = ((), (), s32[]{:S(2)}) async-start(), calls=%async_computation.3 | async-start | bytes 2621440 | tf_op jit(solution)/shard_map/all_gather | solution.py:10
  37.7 78.9 %reduce-scatter.4.cloned.1.call-start = ((), (), s32[]{:S(2)}) async-start(), calls=%async_computation.4 | async-start | bytes 4128768 | tf_op jit(solution)/shard_map/reduce_scatter | solution.py:14
  70.8 5.2 %copy-start = (bf16[2048,896]{1,0:T(8,128)(2,1)S(1)}, bf16[2048,896]{1,0:T(8,128)(2,1)}, u32[]{:S(2)}) copy-start(bf16[2048,896]{1,0:T(8,128)(2,1)} %param.5) | copy-start | bytes 11010052
  70.8 5.2 %copy-start.1 = (bf16[512,2048]{1,0:T(8,128)(2,1)S(1)}, bf16[512,2048]{1,0:T(8,128)(2,1)}, u32[]{:S(2)}) copy-start(bf16[512,2048]{1,0:T(8,128)(2,1)} %all-gather.2.cloned.1.call-done) | copy-start | bytes 6291460
  80.4 110.0 %reduce-scatter.6.cloned.1.call-start = ((), (), s32[]{:S(2)}) async-start(), calls=%async_computation.5 | async-start | bytes 5242880 | tf_op jit(solution)/shard_map/reduce_scatter | solution.py:18
  139.1 92.3 %reduce-scatter.8.cloned.1.call-start = ((), (), s32[]{:S(2)}) async-start(), calls=%async_computation.6 | async-start | bytes 1179648 | tf_op jit(solution)/shard_map/reduce_scatter | solution.py:19
Sparse Core Ops, SparseCore 0:
  37.8 32.9 all-gather.1
  80.5 35.9 reduce-scatter.3
  139.2 51.1 reduce-scatter.5
  192.9 38.3 reduce-scatter.7
where the time goes:
time: 240 us; the launch traced here: 239 us
  waiting for transfers between devices  161 us (67%)
  blocking collectives  46.2 us (19%)
  matrix products  13.8 us (6%)
  between operations  13.2 us (6%)
  other arithmetic  4.72 us (2%)
    reduce_scatter x1, waiting for transfers between devices, on_device(): lax.psum_scatter(partial_out, 'hy', scatter_dimension=0, tiled=True)  51.3 us
    reduce_scatter x1, waiting for transfers between devices, on_device(): totals = lax.psum_scatter(totals, 'hz', scatter_dimension=0, tiled=True)  40.9 us
    reduce_scatter x1, waiting for transfers between devices, on_device(): lax.psum_scatter(partial_value, 'embed', scatter_dimension=0, tiled=True)  36.1 us
    all_gather x1, waiting for transfers between devices, on_device(): piece = lax.all_gather(piece, 'hy', axis=0, tiled=True)  33.1 us
    all_gather x1, blocking collectives, on_device(): piece = lax.all_gather(rows_in, 'hz', axis=0, tiled=True)  31.1 us
    all_gather x1, blocking collectives, on_device(): activated = lax.all_gather(activated, 'embed', axis=0, tiled=True)  15.1 us
    dot_general x1, matrix products, on_device(): jnp.dot(activated, down_weight, preferred_element_type=jnp.float32)  6.35 us
    dot_general x1, matrix products, on_device(): up_part = jnp.dot(piece, up_weight, preferred_element_type=jnp.float32)  5.14 us
  transfers between devices with their start and end apart: 4, of which 4 were waited for; matrix products, arithmetic and copies ran while one was open for 0% of the time, Pallas kernels for 0%

commit v1 on v0

--- a/solution.py
+++ b/solution.py
@@ -4,7 +4,33 @@
 from jax.sharding import Mesh, PartitionSpec as P
 
 
+def _remake_zone(sheet, at_axis):
+    seen_now = list(sheet.shape[1:])
+    seen_now[at_axis] *= sheet.shape[0]
+    return jnp.moveaxis(sheet, 0, at_axis).reshape(seen_now)
+
+
 def on_device(rows_in, gate_weight, up_weight, down_weight):
+
+    def extend_sheets(piece_in, mesh_dim, dim_no):
+        world_n = lax.axis_size(mesh_dim)
+        log = [(kk, (kk + 1) % world_n) for kk in range(world_n)]
+        h_now, value_now = ([], [])
+        blocks_here = [(i, pp) for pp, i in log]
+        for idx in [*range(world_n - 1)]:
+            if idx % 2 == 0:
+                item_now = lax.ppermute(h_now[-1] if h_now else piece_in, mesh_dim, log)
+                h_now.append(item_now)
+            else:
+                value_now.append(
+                    lax.ppermute(value_now[-1] if value_now else piece_in, mesh_dim, blocks_here)
+                )
+        t_next = jnp.stack([*h_now[::-1], piece_in, *value_now])
+        work_now = lax.axis_index(mesh_dim)
+        o_now = work_now - len(h_now)
+        t_next = t_next[(jnp.arange(world_n) - o_now) % world_n]
+        return _remake_zone(t_next, dim_no)
+
     width = gate_weight.shape[1]
     piece = lax.all_gather(rows_in, "hz", axis=0, tiled=True)
     piece = lax.all_gather(piece, "hy", axis=0, tiled=True)
@@ -13,7 +39,7 @@
     partial_value = jnp.concatenate([gate_part, up_part], axis=1)
     summed = lax.psum_scatter(partial_value, "embed", scatter_dimension=0, tiled=True)
     activated = (jax.nn.silu(summed[:, :width]) * summed[:, width:]).astype(jnp.bfloat16)
-    activated = lax.all_gather(activated, "embed", axis=0, tiled=True)
+    activated = extend_sheets(activated, "embed", 0)
     partial_out = jnp.dot(activated, down_weight, preferred_element_type=jnp.float32)
     totals = lax.psum_scatter(partial_out, "hy", scatter_dimension=0, tiled=True)
     totals = lax.psum_scatter(totals, "hz", scatter_dimension=0, tiled=True)

time: 240 us -> 250 us (1.042)
  waiting for transfers between devices: 161 us -> 178 us
  blocking collectives: 46.2 us -> 31.1 us
  starting transfers between devices: 0.13 us -> 7.03 us
    all_gather x1 -> x0, blocking collectives: 15.1 us -> none  [on_device(): activated = lax.all_gather(activated, 'embed', axis=0, tiled=True)]
    ppermute x0 -> x7, waiting for transfers between devices: none -> 11.3 us  [the longest x4 11.3 us: extend_sheets(): item_now = lax.ppermute(h_now[-1] if h_now else piece_in, mesh_dim, log)]
    ppermute x0 -> x7, starting transfers between devices: none -> 6.91 us  [the longest x3 6.88 us: extend_sheets(): lax.ppermute(value_now[-1] if value_now else piece_in, mesh_dim, blocks_h...]
    reduce_scatter x1, waiting for transfers between devices: 51.3 us -> 56.4 us  [on_device(): lax.psum_scatter(partial_out, 'hy', scatter_dimension=0, tiled=True)]
    dot_general x1, matrix products: 2.33 us -> 5.14 us  [on_device(): gate_part = jnp.dot(piece, gate_weight, preferred_element_type=jnp.float32)]
    dot_general x1, matrix products: 5.14 us -> 2.33 us  [on_device(): up_part = jnp.dot(piece, up_weight, preferred_element_type=jnp.float32)]
  transfers between devices with their start and end apart: 4 -> 11, of which waited for: 4 -> 8; matrix products, arithmetic and copies ran while one was open for 0% -> 1% of each run, Pallas kernels for 0% -> 0%
where the time goes in v1:
time: 250 us
  waiting for transfers between devices  178 us (71%)
  blocking collectives  31.1 us (12%)
  matrix products  13.8 us (6%)
  between operations  13.2 us (5%)
  starting transfers between devices  7.03 us (3%)
  other arithmetic  5.88 us (2%)
    reduce_scatter x1, waiting for transfers between devices, on_device(): lax.psum_scatter(partial_out, 'hy', scatter_dimension=0, tiled=True)  56.4 us
    reduce_scatter x1, waiting for transfers between devices, on_device(): totals = lax.psum_scatter(totals, 'hz', scatter_dimension=0, tiled=True)  41 us
    reduce_scatter x1, waiting for transfers between devices, on_device(): lax.psum_scatter(partial_value, 'embed', scatter_dimension=0, tiled=True)  36.1 us
    all_gather x1, waiting for transfers between devices, on_device(): piece = lax.all_gather(piece, 'hy', axis=0, tiled=True)  33.1 us
    all_gather x1, blocking collectives, on_device(): piece = lax.all_gather(rows_in, 'hz', axis=0, tiled=True)  31.1 us
    ppermute x4, waiting for transfers between devices, extend_sheets(): item_now = lax.ppermute(h_now[-1] if h_now else piece_in, mesh_dim, log)  11.3 us
    ppermute x3, starting transfers between devices, extend_sheets(): lax.ppermute(value_now[-1] if value_now else piece_in, mesh_dim, blocks_h...  6.88 us
    dot_general x1, matrix products, on_device(): jnp.dot(activated, down_weight, preferred_element_type=jnp.float32)  6.38 us
  transfers between devices with their start and end apart: 11, of which 8 were waited for; matrix products, arithmetic and copies ran while one was open for 1% of the time, Pallas kernels for 0%

profile of v1, /device:TPU:2, one launch (start us, length us, event | category | flops | bytes accessed | tf_op | source)
XLA Modules:
  0.0 249.9 jit_solution(2500144262496533329)
XLA Ops:
  6.5 31.1 %all_gather.6 = bf16[128,2048]{1,0:T(8,128)(2,1)} all-gather(bf16[16,2048]{1,0:T(8,128)(2,1)} %param.4), channel_id=1, replica_groups=mesh['embed'=8,'hy'=4,'hz'=8] {'hz'}, dimensions={0}, use_global_device_ids=true | all-gather | bytes 589824 | tf_op jit(solution)/shard_map/all_gather | solution.py:35
  37.6 0.0 all-gather.2.cloned.1.call-update
  37.7 0.0 reduce-scatter.4.cloned.1.call-start
  37.7 33.1 %all-gather.2.cloned.1.call-done = bf16[512,2048]{1,0:T(8,128)(2,1)} async-done(((bf16[128,2048]{1,0:T(8,128)(2,1)}), bf16[512,2048]{1,0:T(8,128)(2,1)}) %all-gather.2.cloned.1.call-update) | async-done | bytes 2097168 | tf_op jit(solution)/shard_map/all_gather | solution.py:36
  70.8 5.1 %fusion.3 = f32[512,896]{1,0:T(8,128)S(1)} fusion(bf16[512,2048]{1,0:T(8,128)(2,1)} %all-gather.2.cloned.1.call-done, bf16[2048,896]{1,0:T(8,128)(2,1)} %param.5), kind=kOutput, calls=%fused_computation.19 | convolution fusion | flops 1879048192 | bytes 7602176 | tf_op jit(solution)/shard_map/dot_general | solution.py:37
  76.0 2.3 fusion.4
  78.3 2.1 pad_maximum_fusion
  80.4 0.0 reduce-scatter.6.cloned.1.call-start
  80.4 36.1 %reduce-scatter.4.cloned.1.call-done = f32[64,1792]{1,0:T(8,128)} async-done(((f32[512,1792]{1,0:T(8,128)}), f32[64,1792]{1,0:T(8,128)}) %reduce-scatter.4.cloned.1.call-update) | async-done | bytes 458768 | tf_op jit(solution)/shard_map/reduce_scatter | solution.py:40
  116.5 1.1 fusion
  117.7 4.2 %collective-permute-done = bf16[64,896]{1,0:T(8,128)(2,1)S(1)} collective-permute-done((bf16[64,896]{1,0:T(8,128)(2,1)S(1)}, bf16[64,896]{1,0:T(8,128)(2,1)S(1)}, u32[]{:S(2)}, u32[]{:S(2)}) %collective-permute-start) | collective-permute-done | bytes 114720 | tf_op jit(solution)/shard_map/ppermute | solution.py:22
  121.9 1.7 collective-permute-start.4
  123.6 2.5 collective-permute-done.1
  126.1 2.1 collective-permute-start.5
  128.2 2.3 collective-permute-done.2
  130.5 3.1 %collective-permute-start.6 = (bf16[64,896]{1,0:T(8,128)(2,1)S(1)}, bf16[64,896]{1,0:T(8,128)(2,1)S(1)}, u32[]{:S(2)}, u32[]{:S(2)}) collective-permute-start(bf16[64,896]{1,0:T(8,128)(2,1)S(1)} %collective-permute-done.5), channel_id=1, source_target_pairs={{32,0},{64,32},{96,64},{128,96},{160,128},{192,160},{224,192},{0,2... | collective-permute-start | bytes 344072 | tf_op jit(solution)/shard_map/ppermute | solution.py:26
  133.6 2.3 collective-permute-done.3
  136.0 1.1 bitcast_dynamic-update-slice_fusion.3
  137.2 0.7 gather_fusion
  137.9 6.4 %fusion.5 = f32[512,2048]{1,0:T(8,128)} fusion(bf16[512,896]{1,0:T(8,128)(2,1)S(1)} %bitcast.25, bf16[896,2048]{1,0:T(8,128)(2,1)} %param.7), kind=kOutput, calls=%fused_computation.21 | convolution fusion | flops 1879048192 | bytes 8781824 | tf_op jit(solution)/shard_map/dot_general | solution.py:43
  144.3 0.0 reduce-scatter.8.cloned.1.call-start
  144.4 56.4 %reduce-scatter.6.cloned.1.call-done = f32[128,2048]{1,0:T(8,128)} async-done(((f32[512,2048]{1,0:T(8,128)}), f32[128,2048]{1,0:T(8,128)}) %reduce-scatter.6.cloned.1.call-update) | async-done | bytes 1048592 | tf_op jit(solution)/shard_map/reduce_scatter | solution.py:44
  200.8 41.0 %reduce-scatter.8.cloned.1.call-done = f32[16,2048]{1,0:T(8,128)} async-done(((f32[128,2048]{1,0:T(8,128)}), f32[16,2048]{1,0:T(8,128)}) %reduce-scatter.8.cloned.1.call-update) | async-done | bytes 131088 | tf_op jit(solution)/shard_map/reduce_scatter | solution.py:45
  241.8 1.5 convert_element_type.7
  (24 shorter events, 0.2 us)
Async XLA Ops:
  6.5 64.2 %all-gather.2.cloned.1.call-start = ((), (), s32[]{:S(2)}) async-start(), calls=%async_computation.3 | async-start | bytes 2621440 | tf_op jit(solution)/shard_map/all_gather | solution.py:36
  37.7 78.9 %reduce-scatter.4.cloned.1.call-start = ((), (), s32[]{:S(2)}) async-start(), calls=%async_computation.4 | async-start | bytes 4128768 | tf_op jit(solution)/shard_map/reduce_scatter | solution.py:40
  70.8 5.2 %copy-start = (bf16[2048,896]{1,0:T(8,128)(2,1)S(1)}, bf16[2048,896]{1,0:T(8,128)(2,1)}, u32[]{:S(2)}) copy-start(bf16[2048,896]{1,0:T(8,128)(2,1)} %param.6) | copy-start | bytes 11010052
  70.8 5.2 %copy-start.1 = (bf16[512,2048]{1,0:T(8,128)(2,1)S(1)}, bf16[512,2048]{1,0:T(8,128)(2,1)}, u32[]{:S(2)}) copy-start(bf16[512,2048]{1,0:T(8,128)(2,1)} %all-gather.2.cloned.1.call-done) | copy-start | bytes 6291460
  80.4 120.4 %reduce-scatter.6.cloned.1.call-start = ((), (), s32[]{:S(2)}) async-start(), calls=%async_computation.5 | async-start | bytes 5242880 | tf_op jit(solution)/shard_map/reduce_scatter | solution.py:44
  117.6 4.2 %collective-permute-start = (bf16[64,896]{1,0:T(8,128)(2,1)S(1)}, bf16[64,896]{1,0:T(8,128)(2,1)S(1)}, u32[]{:S(2)}, u32[]{:S(2)}) collective-permute-start(bf16[64,896]{1,0:T(8,128)(2,1)S(1)} %fusion), channel_id=1, source_target_pairs={{0,32},{32,64},{64,96},{96,128},{128,160},{160,192},{192,224},{224... | collective-permute-start | bytes 344072 | tf_op jit(solution)/shard_map/ppermute | solution.py:22
  121.9 4.2 %collective-permute-start.1 = (bf16[64,896]{1,0:T(8,128)(2,1)S(1)}, bf16[64,896]{1,0:T(8,128)(2,1)S(1)}, u32[]{:S(2)}, u32[]{:S(2)}) collective-permute-start(bf16[64,896]{1,0:T(8,128)(2,1)S(1)} %collective-permute-done), channel_id=1, source_target_pairs={{0,32},{32,64},{64,96},{96,128},{128,160},{160,192},{192,224},{224... | collective-permute-start | bytes 344072 | tf_op jit(solution)/shard_map/ppermute | solution.py:22
  121.9 4.2 %collective-permute-start.4 = (bf16[64,896]{1,0:T(8,128)(2,1)S(1)}, bf16[64,896]{1,0:T(8,128)(2,1)S(1)}, u32[]{:S(2)}, u32[]{:S(2)}) collective-permute-start(bf16[64,896]{1,0:T(8,128)(2,1)S(1)} %fusion), channel_id=1, source_target_pairs={{32,0},{64,32},{96,64},{128,96},{160,128},{192,160},{224,192},{0,2... | collective-permute-start | bytes 344072 | tf_op jit(solution)/shard_map/ppermute | solution.py:26
  126.1 4.4 %collective-permute-start.2 = (bf16[64,896]{1,0:T(8,128)(2,1)S(1)}, bf16[64,896]{1,0:T(8,128)(2,1)S(1)}, u32[]{:S(2)}, u32[]{:S(2)}) collective-permute-start(bf16[64,896]{1,0:T(8,128)(2,1)S(1)} %collective-permute-done.1), channel_id=1, source_target_pairs={{0,32},{32,64},{64,96},{96,128},{128,160},{160,192},{192,224},{224... | collective-permute-start | bytes 344072 | tf_op jit(solution)/shard_map/ppermute | solution.py:22
  126.1 4.4 %collective-permute-start.5 = (bf16[64,896]{1,0:T(8,128)(2,1)S(1)}, bf16[64,896]{1,0:T(8,128)(2,1)S(1)}, u32[]{:S(2)}, u32[]{:S(2)}) collective-permute-start(bf16[64,896]{1,0:T(8,128)(2,1)S(1)} %collective-permute-done.4), channel_id=1, source_target_pairs={{32,0},{64,32},{96,64},{128,96},{160,128},{192,160},{224,192},{0,2... | collective-permute-start | bytes 344072 | tf_op jit(solution)/shard_map/ppermute | solution.py:26
  130.5 5.4 %collective-permute-start.3 = (bf16[64,896]{1,0:T(8,128)(2,1)S(1)}, bf16[64,896]{1,0:T(8,128)(2,1)S(1)}, u32[]{:S(2)}, u32[]{:S(2)}) collective-permute-start(bf16[64,896]{1,0:T(8,128)(2,1)S(1)} %collective-permute-done.2), channel_id=1, source_target_pairs={{0,32},{32,64},{64,96},{96,128},{128,160},{160,192},{192,224},{224... | collective-permute-start | bytes 344072 | tf_op jit(solution)/shard_map/ppermute | solution.py:22
  130.5 6.6 %collective-permute-start.6 = (bf16[64,896]{1,0:T(8,128)(2,1)S(1)}, bf16[64,896]{1,0:T(8,128)(2,1)S(1)}, u32[]{:S(2)}, u32[]{:S(2)}) collective-permute-start(bf16[64,896]{1,0:T(8,128)(2,1)S(1)} %collective-permute-done.5), channel_id=1, source_target_pairs={{32,0},{64,32},{96,64},{128,96},{160,128},{192,160},{224,192},{0,2... | collective-permute-start | bytes 344072 | tf_op jit(solution)/shard_map/ppermute | solution.py:26
  144.3 97.5 %reduce-scatter.8.cloned.1.call-start = ((), (), s32[]{:S(2)}) async-start(), calls=%async_computation.6 | async-start | bytes 1179648 | tf_op jit(solution)/shard_map/reduce_scatter | solution.py:45
Sparse Core Ops, SparseCore 0:
  37.8 32.9 all-gather.1
  80.5 35.9 reduce-scatter.3
  144.4 56.3 reduce-scatter.5
  203.4 38.3 reduce-scatter.7
